TPU v7x, 256 devices: a whole 4x4x8 slice. The times are simulated.
256 devices in a mesh: rep: 2 (over y_hi), fsdp: 64 (over x, z, y_lo), tp: 2 (over core).
Axes of the slice: x: 4, y: 4 (y_hi: 2, y_lo: 2; y = y_hi * 2 + y_lo), z: 8, core: 2. Of those that a mesh axis runs over, the one named last changes fastest.
Arguments:
- attn_global: float32 [24, 1024, 1024], P('rep', 'fsdp', 'tp'), may hold values from -6 to 6
- attn_momentum: float32 [24, 1024, 1024], P('rep', 'fsdp', 'tp'), may hold values from -6 to 6
- attn_inner: bfloat16 [2, 24, 1024, 1024], P('rep', None, 'fsdp', 'tp'), may hold values from -6 to 6
- norm_global: float32 [4, 1024], P('rep', 'tp'), may hold values from 0.5 to 1.5
- norm_momentum: float32 [4, 1024], P('rep', 'tp'), may hold values from -4 to 4
- norm_inner: bfloat16 [2, 4, 1024], P('rep', None, 'tp'), may hold values from 0.5 to 1.5
- emb_global: float32 [64, 2, 251, 1024], P('fsdp', 'rep', None, 'tp'), may hold values from -6 to 6
- emb_momentum: float32 [64, 2, 251, 1024], P('fsdp', 'rep', None, 'tp'), may hold values from -6 to 6
- emb_inner: bfloat16 [2, 32128, 1024], P('rep', 'fsdp', 'tp'), may hold values from -6 to 6
- basis: float32 [1024, 64], replicated, may hold values from -0.1875 to 0.1875
- touched: int32 [2, 8192], replicated, may hold values from 0 to 32127
Outputs:
- new_attn_global: float32 [24, 1024, 1024], P('rep', 'fsdp', 'tp')
- new_attn_momentum: float32 [24, 1024, 1024], P('rep', 'fsdp', 'tp')
- attn_weights: float32 [24, 1024, 1024], P(None, 'fsdp', 'tp')
- new_norm_global: float32 [4, 1024], P('rep', 'tp')
- new_norm_momentum: float32 [4, 1024], P('rep', 'tp')
- norm_weights: float32 [4, 1024], P(None, 'tp')
- new_emb_global: float32 [64, 2, 251, 1024], P('fsdp', 'rep', None, 'tp')
- new_emb_momentum: float32 [64, 2, 251, 1024], P('fsdp', 'rep', None, 'tp')
- emb_weights: float32 [32128, 1024], P('fsdp', 'tp')
All inputs are finite; a program needn't handle non-finite values.
Results may differ from a plain program's by a relative error of at most 0.0003.
Values sent between devices are 32-bit elements; how exact they have to be, the bound alone decides.
No kernel may reach another device: no remote copies, remote signals or barrier semaphores. Data moves between devices by JAX's collectives and lax.ppermute only.
A program may use at most 64 MiB of HBM per device.

v0:
```python
import jax
import jax.numpy as jnp
from jax import lax
from jax.sharding import PartitionSpec as P

OUTER_RATE = 0.7
MOMENTUM = 0.9


def nesterov(global_part, momentum_part, outer_grad):
    fresh_momentum = MOMENTUM * momentum_part + outer_grad
    fresh_global = global_part - OUTER_RATE * (outer_grad + MOMENTUM * fresh_momentum)
    return (fresh_global, fresh_momentum)


def per_device(
    attn_global,
    attn_momentum,
    attn_inner,
    norm_global,
    norm_momentum,
    norm_inner,
    emb_global,
    emb_momentum,
    emb_inner,
    basis,
    touched,
):
    groups = lax.axis_size("rep") * 1.0
    rep_index = lax.axis_index("rep")
    attn_terms = attn_inner[0].astype(jnp.float32)
    norm_terms = norm_inner[0].astype(jnp.float32)
    attn_total, norm_total = lax.psum((attn_terms, norm_terms), "rep")
    attn_owned = attn_global.shape[0]
    norm_owned = norm_global.shape[0]
    attn_summed = lax.dynamic_slice_in_dim(attn_total, rep_index * attn_owned, attn_owned, 0)
    norm_summed = lax.dynamic_slice_in_dim(norm_total, rep_index * norm_owned, norm_owned, 0)
    new_attn_global, new_attn_momentum = nesterov(
        attn_global, attn_momentum, attn_global - attn_summed / groups
    )
    new_norm_global, new_norm_momentum = nesterov(
        norm_global, norm_momentum, norm_global - norm_summed / groups
    )
    block_rows = emb_inner.shape[1]
    half_rows = emb_global.shape[2]
    half_width = emb_global.shape[3]
    row_start = lax.axis_index("fsdp") * block_rows
    half_start = rep_index * half_rows
    positions = row_start + jnp.arange(block_rows, dtype=jnp.int32)
    matches = touched[:, :, None] == positions[None, None, :]
    touched_masks = jnp.any(matches, axis=1).astype(jnp.float32)
    counts = jnp.sum(touched_masks, axis=0)
    own_mask = lax.dynamic_index_in_dim(touched_masks, rep_index, 0, keepdims=False)
    half_counts = lax.dynamic_slice_in_dim(counts, half_start, half_rows, 0)
    basis_half = lax.dynamic_slice_in_dim(basis, lax.axis_index("tp") * half_width, half_width, 0)
    own_rows = emb_global[0, 0]
    own_momentum = emb_momentum[0, 0]
    global_coeff = jnp.dot(
        own_rows, basis_half, precision=lax.Precision.HIGHEST, preferred_element_type=jnp.float32
    )
    placed_global = lax.dynamic_update_slice_in_dim(
        jnp.zeros((block_rows, basis.shape[1]), jnp.float32),
        half_counts[:, None] * global_coeff,
        half_start,
        0,
    )
    inner_coeff = jnp.dot(
        emb_inner[0].astype(jnp.float32),
        basis_half,
        precision=lax.Precision.HIGHEST,
        preferred_element_type=jnp.float32,
    )
    coeff_term = placed_global - own_mask[:, None] * inner_coeff
    coeff_total = lax.psum(coeff_term.reshape(-1), ("rep", "tp")).reshape(coeff_term.shape)
    coeff_sum = lax.dynamic_slice_in_dim(coeff_total, half_start, half_rows, 0)
    emb_grad = (
        jnp.dot(
            coeff_sum,
            basis_half.T,
            precision=lax.Precision.HIGHEST,
            preferred_element_type=jnp.float32,
        )
        / groups
    )
    fresh_rows, fresh_momentum = nesterov(own_rows, own_momentum, emb_grad)
    new_emb_global = fresh_rows.reshape(emb_global.shape)
    new_emb_momentum = fresh_momentum.reshape(emb_momentum.shape)
    attn_weights, norm_weights, emb_halves = (
        lax.all_gather(new_attn_global, "rep", axis=0, tiled=True),
        lax.all_gather(new_norm_global, "rep", axis=0, tiled=True),
        lax.all_gather(new_emb_global, "rep", axis=1, tiled=True),
    )
    emb_weights = emb_halves.reshape(block_rows, half_width)
    return (
        new_attn_global,
        new_attn_momentum,
        attn_weights,
        new_norm_global,
        new_norm_momentum,
        norm_weights,
        new_emb_global,
        new_emb_momentum,
        emb_weights,
    )


def solution(mesh):
    placed = (
        P("rep", "fsdp", "tp"),
        P("rep", "fsdp", "tp"),
        P("rep", None, "fsdp", "tp"),
        P("rep", "tp"),
        P("rep", "tp"),
        P("rep", None, "tp"),
        P("fsdp", "rep", None, "tp"),
        P("fsdp", "rep", None, "tp"),
        P("rep", "fsdp", "tp"),
        P(),
        P(),
    )
    return jax.shard_map(
        per_device,
        mesh=mesh,
        in_specs=placed,
        out_specs=(
            P("rep", "fsdp", "tp"),
            P("rep", "fsdp", "tp"),
            P(None, "fsdp", "tp"),
            P("rep", "tp"),
            P("rep", "tp"),
            P(None, "tp"),
            P("fsdp", "rep", None, "tp"),
            P("fsdp", "rep", None, "tp"),
            P("fsdp", "tp"),
        ),
        check_vma=False,
    )
```

profile of v0, /device:TPU:2, one launch (start us, length us, event | category | flops | bytes accessed | tf_op | source)
XLA Modules:
  0.0 138.5 jit_solution(1538203716766188428)
XLA Ops:
  7.2 0.0 copy-start
  7.2 0.0 copy-start.3
  7.2 0.0 all-reduce.5.cloned.1.call-start
  7.3 5.2 %compare_reduce_fusion = pred[2,502]{1,0:T(4,128)(4,1)S(1)} fusion(s32[2,8192]{1,0:T(2,128)} %param.21, s32[502]{0:T(512)S(1)} %iota_add_fusion), kind=kLoop, calls=%fused_computation | loop fusion | flops 16448532 | bytes 68548 | tf_op jit(solution)/shard_map/reduce_or | solution.py:51
  12.5 0.0 copy-start.5
  12.5 0.1 dynamic_slice.21
  12.6 1.7 %fusion.2 = f32[251,64]{0,1:T(8,128)S(1)} fusion(f32[1,1,251,512]{3,1,2,0:T(1,128)} %param.17, f32[1024,64]{0,1:T(8,128)} %param.20, s32[]{:T(128)S(6)} %select_n.21, f32[251]{0:T(256)S(1)} %dynamic_slice.21), kind=kOutput, calls=%fused_computation.6 | convolution fusion | flops 98713280 | bytes 710384 | tf_op jit(solution)/shard_map/dot_general | solution.py:58
  14.3 0.7 dynamic_update_slice.3
  15.0 1.3 fusion.1
  16.3 0.0 all-reduce.5.cloned.1.call-update
  16.3 0.0 copy-start.1
  16.3 0.0 copy-start.4
  16.3 0.0 all-reduce.3.cloned.1.call-start
  16.4 1.0 bitcast_convert_fusion
  17.4 0.0 all-reduce.3.cloned.1.call-update
  17.4 0.0 copy-done.9
  17.4 6.5 %psum.22 = f32[4,512]{1,0:T(4,128)S(1)} all-reduce(f32[4,512]{1,0:T(4,128)S(1)} %bitcast_convert_fusion.1), channel_id=1, replica_groups=mesh['rep'=2,'fsdp'=64,'tp'=2] {'rep'}, use_global_device_ids=true, to_apply=%region_1.0 | all-reduce | flops 2048 | bytes 16384 | tf_op jit(solution)/shard_map/psum | solution.py:33
  23.9 0.0 copy-done.10
  23.9 0.6 multiply_subtract_fusion.2
  24.6 5.9 %all-gather.1 = f32[2,2,512]{2,1,0:T(2,128)S(1)} all-gather(f32[1,2,512]{2,1,0:T(2,128)S(1)} %bitcast.41), channel_id=1, replica_groups=mesh['rep'=2,'fsdp'=64,'tp'=2] {'rep'}, dimensions={0}, use_global_device_ids=true | all-gather | bytes 12288 | tf_op jit(solution)/shard_map/all_gather | solution.py:90
  30.4 0.6 reshape.58
  31.0 33.8 %all-reduce.5.cloned.1.call-done = f32[502,64]{0,1:T(8,128)} async-done(((f32[502,64]{0,1:T(8,128)}), f32[502,64]{0,1:T(8,128)}) %all-reduce.5.cloned.1.call-update) | async-done | bytes 128528 | tf_op jit(solution)/shard_map/psum | solution.py:74
  64.8 1.7 %fusion.14 = (f32[1,251,512]{2,1,0:T(8,128)S(1)}, f32[1,1,251,512]{3,2,1,0:T(8,128)S(1)}, f32[1,1,251,512]{3,2,1,0:T(8,128)S(1)}) fusion(f32[1,1,251,512]{3,1,2,0:T(1,128)S(1)} %copy-done.4, f32[1,1,251,512]{3,1,2,0:T(1,128)S(1)} %copy-done.1, f32[1024,64]{0,1:T(8,128)S(1)} %copy-done.3, s32[]{:T(128)S(6)} %select_n.21, ...), kind=kOutput, calls=%fused_computation.32 | convolution fusion | flops 99596800 | bytes 2766856 | tf_op jit(solution)/shard_map/dot_general | solution.py:77
  66.6 0.0 copy-done.8
  66.6 17.8 %all-gather.2 = f32[2,251,512]{2,1,0:T(8,128)S(1)} all-gather(f32[1,251,512]{2,1,0:T(8,128)S(1)} %get-tuple-element.49), channel_id=2, replica_groups=mesh['rep'=2,'fsdp'=64,'tp'=2] {'rep'}, dimensions={0}, use_global_device_ids=true | all-gather | bytes 1542144 | tf_op jit(solution)/shard_map/all_gather | solution.py:91
  84.4 1.1 reshape.60
  85.5 1.3 copy.30
  86.8 1.3 copy.31
  88.1 27.9 %all-reduce.3.cloned.1.call-done = f32[24,16,512]{2,1,0:T(8,128)} async-done(((f32[24,16,512]{2,1,0:T(8,128)}), f32[24,16,512]{2,1,0:T(8,128)}) %all-reduce.3.cloned.1.call-update) | async-done | bytes 786448 | tf_op jit(solution)/shard_map/psum | solution.py:33
  116.0 1.9 %multiply_subtract_fusion = (f32[12,16,512]{2,1,0:T(8,128)S(1)}, f32[12,16,512]{2,1,0:T(8,128)}) fusion(f32[12,16,512]{2,1,0:T(8,128)S(1)} %copy-done.6, f32[24,16,512]{2,1,0:T(8,128)} %all-reduce.3.cloned.1.call-done, s32[]{:T(128)S(6)} %select_n.18, f32[12,16,512]{2,1,0:T(8,128)S(1)} %copy-done.7), kind=kLoop, calls=%fused_computation.14 | loop fusion | flops 786432 | bytes 1966084 | tf_op jit(solution)/shard_map/sub | solution.py:12
  117.9 12.8 %all_gather.9 = f32[24,16,512]{2,1,0:T(8,128)S(1)} all-gather(f32[12,16,512]{2,1,0:T(8,128)S(1)} %get-tuple-element.61), channel_id=1, replica_groups=mesh['rep'=2,'fsdp'=64,'tp'=2] {'rep'}, dimensions={0}, use_global_device_ids=true | all-gather | bytes 1179648 | tf_op jit(solution)/shard_map/all_gather | solution.py:89
  130.8 0.9 copy.57
  (22 shorter events, 0.1 us)
Async XLA Ops:
  7.2 7.8 %copy-start = (bf16[1,502,512]{2,1,0:T(8,128)(2,1)S(1)}, bf16[1,502,512]{2,1,0:T(8,128)(2,1)}, u32[]{:S(2)}) copy-start(bf16[1,502,512]{2,1,0:T(8,128)(2,1)} %param.19) | copy-start | bytes 1542148
  7.2 7.8 %copy-start.3 = (f32[1024,64]{0,1:T(8,128)S(1)}, f32[1024,64]{0,1:T(8,128)}, u32[]{:S(2)}) copy-start(f32[1024,64]{0,1:T(8,128)} %param.20) | copy-start | bytes 786436
  7.2 57.6 %all-reduce.5.cloned.1.call-start = ((), (), s32[]{:S(2)}) async-start(), calls=%async_computation.1 | async-start | bytes 262144 | tf_op jit(solution)/shard_map/psum | solution.py:74
  12.5 3.9 %copy-start.5 = (bf16[1,24,16,512]{3,2,1,0:T(8,128)(2,1)S(1)}, bf16[1,24,16,512]{3,2,1,0:T(8,128)(2,1)}, u32[]{:S(2)}) copy-start(bf16[1,24,16,512]{3,2,1,0:T(8,128)(2,1)} %param.13) | copy-start | bytes 1179652
  16.3 1.1 copy-start.9
  16.3 7.6 %copy-start.10 = (f32[2,512]{1,0:T(2,128)S(1)}, f32[2,512]{1,0:T(2,128)}, u32[]{:S(2)}) copy-start(f32[2,512]{1,0:T(2,128)} %param.14) | copy-start | bytes 12292
  16.3 7.6 %copy-start.11 = (f32[2,512]{1,0:T(2,128)S(1)}, f32[2,512]{1,0:T(2,128)}, u32[]{:S(2)}) copy-start(f32[2,512]{1,0:T(2,128)} %param.15) | copy-start | bytes 12292
  16.3 48.5 %copy-start.1 = (f32[1,1,251,512]{3,1,2,0:T(1,128)S(1)}, f32[1,1,251,512]{3,1,2,0:T(1,128)}, u32[]{:S(2)}) copy-start(f32[1,1,251,512]{3,1,2,0:T(1,128)} %param.17) | copy-start | bytes 1542148
  16.3 48.5 %copy-start.4 = (f32[1,1,251,512]{3,1,2,0:T(1,128)S(1)}, f32[1,1,251,512]{3,1,2,0:T(1,128)}, u32[]{:S(2)}) copy-start(f32[1,1,251,512]{3,1,2,0:T(1,128)} %param.18) | copy-start | bytes 1542148
  16.3 99.7 %all-reduce.3.cloned.1.call-start = ((), (), s32[]{:S(2)}) async-start(), calls=%async_computation | async-start | bytes 1572864 | tf_op jit(solution)/shard_map/psum | solution.py:33
  24.6 42.0 %copy-start.8 = (f32[2,512]{1,0:T(2,128)}, f32[2,512]{1,0:T(2,128)S(1)}, u32[]{:S(2)}) copy-start(f32[2,512]{1,0:T(2,128)S(1)} %get-tuple-element.64) | copy-start | bytes 12292
  85.5 30.6 %copy-start.6 = (f32[12,16,512]{2,1,0:T(8,128)S(1)}, f32[12,16,512]{2,1,0:T(8,128)}, u32[]{:S(2)}) copy-start(f32[12,16,512]{2,1,0:T(8,128)} %param.11) | copy-start | bytes 1179652
  85.5 30.6 %copy-start.7 = (f32[12,16,512]{2,1,0:T(8,128)S(1)}, f32[12,16,512]{2,1,0:T(8,128)}, u32[]{:S(2)}) copy-start(f32[12,16,512]{2,1,0:T(8,128)} %param.12) | copy-start | bytes 1179652
  117.9 13.7 %copy-start.2 = (f32[12,16,512]{2,1,0:T(8,128)}, f32[12,16,512]{2,1,0:T(8,128)S(1)}, u32[]{:S(2)}) copy-start(f32[12,16,512]{2,1,0:T(8,128)S(1)} %get-tuple-element.61) | copy-start | bytes 1179652
Sparse Core Ops, SparseCore 0:
  16.4 48.3 all-reduce.4
  68.0 47.9 all-reduce.2
where the time goes:
time: 139 us; the launch traced here: 138 us
  waiting for transfers between devices  61.8 us (44%)
  blocking collectives  43 us (31%)
  between operations  14.2 us (10%)
  other arithmetic  8.68 us (6%)
  local copies, waits for them, and re-layouts  6 us (4%)
  matrix products  4.69 us (3%)
    psum x1, waiting for transfers between devices, per_device(): lax.psum(coeff_term.reshape(-1), ('rep', 'tp')).reshape(coeff_term.shape)  33.8 us
    psum x1, waiting for transfers between devices, per_device(): attn_total, norm_total = lax.psum((attn_terms, norm_terms), 'rep')  27.9 us
    all_gather x1, blocking collectives, per_device(): lax.all_gather(new_emb_global, 'rep', axis=1, tiled=True)  17.8 us
    all_gather x1, blocking collectives, per_device(): lax.all_gather(new_attn_global, 'rep', axis=0, tiled=True)  12.8 us
    psum x1, blocking collectives, per_device(): attn_total, norm_total = lax.psum((attn_terms, norm_terms), 'rep')  6.51 us
    all_gather x1, blocking collectives, per_device(): lax.all_gather(new_norm_global, 'rep', axis=0, tiled=True)  5.85 us
    unnamed x29, local copies, waits for them, and re-layouts  5.24 us
    reduce_or x1, other arithmetic, per_device(): touched_masks = jnp.any(matches, axis=1).astype(jnp.float32)  5.18 us
  transfers between devices with their start and end apart: 2, of which 2 were waited for; matrix products, arithmetic and copies ran while one was open for 5% of the time, Pallas kernels for 0%

commit v1 on v0

--- a/solution.py
+++ b/solution.py
@@ -71,7 +71,9 @@
         preferred_element_type=jnp.float32,
     )
     coeff_term = placed_global - own_mask[:, None] * inner_coeff
-    coeff_total = lax.psum(coeff_term.reshape(-1), ("rep", "tp")).reshape(coeff_term.shape)
+    coeff_total = jnp.sum(lax.all_gather(coeff_term.reshape(-1), ("rep", "tp")), axis=0).reshape(
+        coeff_term.shape
+    )
     coeff_sum = lax.dynamic_slice_in_dim(coeff_total, half_start, half_rows, 0)
     emb_grad = (
         jnp.dot(

time: 139 us -> 87.5 us (0.63)
  waiting for transfers between devices: 61.8 us -> 0.02 us
  blocking collectives: 43 us -> 54.3 us
  matrix products: 4.69 us -> 2.94 us
    psum x1 -> x0, waiting for transfers between devices: 33.8 us -> none  [per_device(): lax.psum(coeff_term.reshape(-1), ('rep', 'tp')).reshape(coeff_term.shape)]
    psum x1, waiting for transfers between devices: 27.9 us -> 0.01 us  [per_device(): attn_total, norm_total = lax.psum((attn_terms, norm_terms), 'rep')]
    all_gather x0 -> x1, blocking collectives: none -> 8.89 us  [per_device(): lax.all_gather(coeff_term.reshape(-1), ('rep', 'tp'))]
    all_gather x1, blocking collectives: 17.8 us -> 21.1 us  [per_device(): lax.all_gather(new_emb_global, 'rep', axis=1, tiled=True)]
    unnamed x29 -> x28, local copies, waits for them, and re-layouts: 5.24 us -> 5.42 us
  transfers between devices with their start and end apart: 2 -> 1, of which waited for: 2 -> 0; matrix products, arithmetic and copies ran while one was open for 5% -> 16% of each run, Pallas kernels for 0% -> 0%
where the time goes in v1:
time: 87.5 us; the launch traced here: 87.3 us
  blocking collectives  54.3 us (62%)
  between operations  14.2 us (16%)
  other arithmetic  9.36 us (11%)
  local copies, waits for them, and re-layouts  6.4 us (7%)
  matrix products  2.94 us (3%)
    all_gather x1, blocking collectives, per_device(): lax.all_gather(new_emb_global, 'rep', axis=1, tiled=True)  21.1 us
    all_gather x1, blocking collectives, per_device(): lax.all_gather(new_attn_global, 'rep', axis=0, tiled=True)  11.7 us
    all_gather x1, blocking collectives, per_device(): lax.all_gather(coeff_term.reshape(-1), ('rep', 'tp'))  8.89 us
    psum x1, blocking collectives, per_device(): attn_total, norm_total = lax.psum((attn_terms, norm_terms), 'rep')  6.79 us
    all_gather x1, blocking collectives, per_device(): lax.all_gather(new_norm_global, 'rep', axis=0, tiled=True)  5.85 us
    unnamed x28, local copies, waits for them, and re-layouts  5.42 us
    reduce_or x1, other arithmetic, per_device(): touched_masks = jnp.any(matches, axis=1).astype(jnp.float32)  4.29 us
    sub x2, other arithmetic, nesterov(): global_part - OUTER_RATE * (outer_grad + MOMENTUM * fresh_momentum)  2.49 us
  transfers between devices with their start and end apart: 1, of which 0 were waited for; matrix products, arithmetic and copies ran while one was open for 16% of the time, Pallas kernels for 0%

profile of v1, /device:TPU:2, one launch (start us, length us, event | category | flops | bytes accessed | tf_op | source)
XLA Modules:
  0.0 87.3 jit_solution(2578945215081955666)
XLA Ops:
  7.2 0.0 copy-start
  7.2 0.0 copy-start.6
  7.2 0.0 copy-start.1
  7.2 0.0 all-reduce.2.cloned.1.call-start
  7.3 2.1 %bitcast_convert_fusion = f32[24,16,512]{2,1,0:T(8,128)} fusion(bf16[1,24,16,512]{3,2,1,0:T(8,128)(2,1)} %param.13), kind=kLoop, calls=%fused_computation.13 | loop fusion | flops 196608 | bytes 1179648 | tf_op jit(solution)/shard_map/convert_element_type | solution.py:31
  9.3 0.0 all-reduce.2.cloned.1.call-update
  9.4 4.3 %compare_reduce_fusion = pred[2,502]{1,0:T(4,128)(4,1)S(1)} fusion(s32[2,8192]{1,0:T(2,128)S(1)} %copy-done.6, s32[502]{0:T(512)S(1)} %iota_add_fusion), kind=kLoop, calls=%fused_computation | loop fusion | flops 16448532 | bytes 68548 | tf_op jit(solution)/shard_map/reduce_or | solution.py:51
  13.7 0.1 dynamic_slice.21
  13.8 0.0 copy-done.3
  13.8 0.6 fusion.2
  14.4 0.7 dynamic_update_slice.3
  15.1 0.6 fusion.1
  15.7 0.1 copy.31
  15.9 0.2 reshape.54
  16.1 8.9 %all-gather.2 = f32[4,1,32128]{2,1,0:T(1,128)S(1)} all-gather(f32[1,1,32128]{2,1,0:T(1,128)S(1)} %reshape.54), channel_id=1, replica_groups=mesh['rep'=2,'fsdp'=64,'tp'=2] {'rep','tp'}, dimensions={0}, use_global_device_ids=true | all-gather | bytes 642560 | tf_op jit(solution)/shard_map/all_gather | solution.py:74
  24.9 0.5 reduce_sum.19
  25.4 0.1 reshape.44
  25.5 1.7 %fusion.14 = (f32[1,251,512]{2,1,0:T(8,128)S(1)}, f32[1,1,251,512]{3,2,1,0:T(8,128)S(1)}, f32[1,1,251,512]{3,2,1,0:T(8,128)S(1)}) fusion(f32[1,1,251,512]{3,1,2,0:T(1,128)} %param.18, f32[1,1,251,512]{3,1,2,0:T(1,128)S(1)} %copy-done.1, f32[1024,64]{0,1:T(8,128)S(1)} %copy-done.3, s32[]{:T(128)S(6)} %select_n.21, f32[502,64]{1,0:T(8,128)S(1)} %reshape.44, ...), kind=kOutput, calls=%fused_computation.32 | convolution fusion | flops 99596800 | bytes 2832392 | tf_op jit(solution)/shard_map/dot_general | solution.py:79
  27.3 21.1 %all-gather.3 = f32[2,251,512]{2,1,0:T(8,128)S(1)} all-gather(f32[1,251,512]{2,1,0:T(8,128)S(1)} %get-tuple-element.49), channel_id=2, replica_groups=mesh['rep'=2,'fsdp'=64,'tp'=2] {'rep'}, dimensions={0}, use_global_device_ids=true | all-gather | bytes 1542144 | tf_op jit(solution)/shard_map/all_gather | solution.py:93
  48.4 1.1 %reshape.57 = f32[502,512]{1,0:T(8,128)} reshape(f32[2,251,512]{2,1,0:T(8,128)S(1)} %all-gather.3) | data formatting | bytes 2056192
  49.4 0.0 copy-start.5
  49.5 1.3 %copy.33 = f32[1,1,251,512]{3,1,2,0:T(1,128)} copy(f32[1,1,251,512]{3,2,1,0:T(8,128)S(1)} %get-tuple-element.50) | data formatting | bytes 1028096
  50.8 1.3 %copy.34 = f32[1,1,251,512]{3,1,2,0:T(1,128)} copy(f32[1,1,251,512]{3,2,1,0:T(8,128)S(1)} %get-tuple-element.51) | data formatting | bytes 1028096
  52.1 6.8 %psum.15 = f32[4,512]{1,0:T(4,128)S(1)} all-reduce(f32[4,512]{1,0:T(4,128)S(1)} %bitcast_convert_fusion.1), channel_id=1, replica_groups=mesh['rep'=2,'fsdp'=64,'tp'=2] {'rep'}, use_global_device_ids=true, to_apply=%region_1.0 | all-reduce | flops 2048 | bytes 16384 | tf_op jit(solution)/shard_map/psum | solution.py:33
  58.9 0.0 copy-done.9
  58.9 0.6 multiply_subtract_fusion.2
  59.5 5.9 %all-gather.1 = f32[2,2,512]{2,1,0:T(2,128)S(1)} all-gather(f32[1,2,512]{2,1,0:T(2,128)S(1)} %bitcast.41), channel_id=1, replica_groups=mesh['rep'=2,'fsdp'=64,'tp'=2] {'rep'}, dimensions={0}, use_global_device_ids=true | all-gather | bytes 12288 | tf_op jit(solution)/shard_map/all_gather | solution.py:92
  65.4 0.6 reshape.53
  66.0 0.0 copy-done.4
  66.0 1.9 %multiply_subtract_fusion = (f32[12,16,512]{2,1,0:T(8,128)S(1)}, f32[12,16,512]{2,1,0:T(8,128)}) fusion(f32[12,16,512]{2,1,0:T(8,128)S(1)} %copy-done.4, f32[24,16,512]{2,1,0:T(8,128)} %all-reduce.2.cloned.1.call-done, s32[]{:T(128)S(6)} %select_n.18, f32[12,16,512]{2,1,0:T(8,128)S(1)} %copy-done.5), kind=kLoop, calls=%fused_computation.14 | loop fusion | flops 786432 | bytes 1966084 | tf_op jit(solution)/shard_map/sub | solution.py:12
  67.9 11.7 %all_gather.12 = f32[24,16,512]{2,1,0:T(8,128)S(1)} all-gather(f32[12,16,512]{2,1,0:T(8,128)S(1)} %get-tuple-element.61), channel_id=1, replica_groups=mesh['rep'=2,'fsdp'=64,'tp'=2] {'rep'}, dimensions={0}, use_global_device_ids=true | all-gather | bytes 1179648 | tf_op jit(solution)/shard_map/all_gather | solution.py:91
  79.5 0.9 %copy.59 = f32[24,16,512]{2,1,0:T(8,128)} copy(f32[24,16,512]{2,1,0:T(8,128)S(1)} %all_gather.12) | data formatting | bytes 1572864
  (22 shorter events, 0.1 us)
Async XLA Ops:
  7.2 7.9 %copy-start = (bf16[1,502,512]{2,1,0:T(8,128)(2,1)S(1)}, bf16[1,502,512]{2,1,0:T(8,128)(2,1)}, u32[]{:S(2)}) copy-start(bf16[1,502,512]{2,1,0:T(8,128)(2,1)} %param.19) | copy-start | bytes 1542148
  7.2 2.2 %copy-start.6 = (s32[2,8192]{1,0:T(2,128)S(1)}, s32[2,8192]{1,0:T(2,128)}, u32[]{:S(2)}) copy-start(s32[2,8192]{1,0:T(2,128)} %param.21) | copy-start | bytes 196612
  7.2 6.6 %copy-start.1 = (f32[1,1,251,512]{3,1,2,0:T(1,128)S(1)}, f32[1,1,251,512]{3,1,2,0:T(1,128)}, u32[]{:S(2)}) copy-start(f32[1,1,251,512]{3,1,2,0:T(1,128)} %param.17) | copy-start | bytes 1542148
  7.2 6.6 %copy-start.3 = (f32[1024,64]{0,1:T(8,128)S(1)}, f32[1024,64]{0,1:T(8,128)}, u32[]{:S(2)}) copy-start(f32[1024,64]{0,1:T(8,128)} %param.20) | copy-start | bytes 786436
  7.2 58.8 %all-reduce.2.cloned.1.call-start = ((), (), s32[]{:S(2)}) async-start(), calls=%async_computation | async-start | bytes 1572864 | tf_op jit(solution)/shard_map/psum | solution.py:33
  49.4 2.7 %copy-start.8 = (bf16[1,4,512]{2,1,0:T(4,128)(2,1)S(1)}, bf16[1,4,512]{2,1,0:T(4,128)(2,1)}, u32[]{:S(2)}) copy-start(bf16[1,4,512]{2,1,0:T(4,128)(2,1)} %param.16) | copy-start | bytes 12292
  49.4 9.4 %copy-start.9 = (f32[2,512]{1,0:T(2,128)S(1)}, f32[2,512]{1,0:T(2,128)}, u32[]{:S(2)}) copy-start(f32[2,512]{1,0:T(2,128)} %param.14) | copy-start | bytes 12292
  49.4 9.4 %copy-start.10 = (f32[2,512]{1,0:T(2,128)S(1)}, f32[2,512]{1,0:T(2,128)}, u32[]{:S(2)}) copy-start(f32[2,512]{1,0:T(2,128)} %param.15) | copy-start | bytes 12292
  49.4 16.5 %copy-start.4 = (f32[12,16,512]{2,1,0:T(8,128)S(1)}, f32[12,16,512]{2,1,0:T(8,128)}, u32[]{:S(2)}) copy-start(f32[12,16,512]{2,1,0:T(8,128)} %param.11) | copy-start | bytes 1179652
  49.4 16.5 %copy-start.5 = (f32[12,16,512]{2,1,0:T(8,128)S(1)}, f32[12,16,512]{2,1,0:T(8,128)}, u32[]{:S(2)}) copy-start(f32[12,16,512]{2,1,0:T(8,128)} %param.12) | copy-start | bytes 1179652
  59.5 20.0 %copy-start.7 = (f32[2,512]{1,0:T(2,128)}, f32[2,512]{1,0:T(2,128)S(1)}, u32[]{:S(2)}) copy-start(f32[2,512]{1,0:T(2,128)S(1)} %get-tuple-element.64) | copy-start | bytes 12292
  67.9 12.6 %copy-start.2 = (f32[12,16,512]{2,1,0:T(8,128)}, f32[12,16,512]{2,1,0:T(8,128)S(1)}, u32[]{:S(2)}) copy-start(f32[12,16,512]{2,1,0:T(8,128)S(1)} %get-tuple-element.61) | copy-start | bytes 1179652
Sparse Core Ops, SparseCore 0:
  11.2 53.4 all-reduce.1
